TPU v7x, 128 devices: a whole 4x4x4 slice. The times are simulated.
128 devices in a mesh: rows: 32 (over x, y, core), dims: 4 (over z).
Axes of the slice: x: 4, y: 4, z: 4, core: 2. Of those that a mesh axis runs over, the one named last changes fastest.
Arguments:
- gradients: float32 [65536, 4096], P('rows', 'dims'), may hold values from -0.5 to 0.5
- ridge: float32 [], replicated, may hold values from 2 to 8
- panel_index: int32 [1], replicated, may hold values from 0 to 63
- block_ids: int32 [64], replicated, may hold values from 0 to 63, each once
Outputs:
- panel: float32 [65536, 1024], P(('rows', 'dims'))
Inputs may be any that keep to these rules, and one draw needn't show every extreme that they name: block_ids is a permutation of the row blocks' numbers.
All inputs are finite; a program needn't handle non-finite values.
Results may differ from a plain program's by a relative error of at most 0.000081.
Values sent between devices are 32-bit elements; how exact they have to be, the bound alone decides.
No kernel may reach another device: no remote copies, remote signals or barrier semaphores. Data moves between devices by JAX's collectives and lax.ppermute only.
A program may use at most 128 MiB of HBM per device.

v0:
```python
import jax
import jax.numpy as jnp
from jax import lax
from jax.experimental import pallas as pl
from jax.experimental.pallas import tpu as pltpu
from jax.sharding import PartitionSpec as P

NB = 128
HI = lax.Precision.HIGHEST


def _dot_t(a, b):
    return lax.dot_general(a, b, (((1,), (1,)), ((), ())), precision=HI, preferred_element_type=jnp.float32)


def _dot_high(a, b):
    return lax.dot_general(
        a, b, (((1,), (1,)), ((), ())), precision=lax.Precision.HIGH, preferred_element_type=jnp.float32
    )


def _dot(a, b):
    return lax.dot_general(a, b, (((1,), (0,)), ((), ())), precision=HI, preferred_element_type=jnp.float32)


def _inv_chol_kernel(a_ref, w_ref, work):
    n = a_ref.shape[0]
    nblk = n // NB
    work[...] = a_ref[...]
    w_ref[...] = jnp.zeros_like(w_ref)
    rid = lax.broadcasted_iota(jnp.int32, (NB, NB), 0)
    cid = lax.broadcasted_iota(jnp.int32, (NB, NB), 1)
    rid1 = lax.broadcasted_iota(jnp.int32, (NB, 1), 0)
    cid1 = lax.broadcasted_iota(jnp.int32, (1, NB), 1)
    eye = jnp.where(rid == cid, 1.0, 0.0).astype(jnp.float32)

    def step(k, carry):
        s, r = carry
        row = jnp.sum(jnp.where(rid == k, s, 0.0), axis=0, keepdims=True)
        col = jnp.sum(jnp.where(cid == k, s, 0.0), axis=1, keepdims=True)
        d = jnp.sum(jnp.where(rid1 == k, col, 0.0), axis=0, keepdims=True)
        inv = lax.rsqrt(d)
        l_row = jnp.where(cid1 >= k, row * inv, 0.0)
        l_col = jnp.where(rid1 >= k, col * inv, 0.0)
        s = s - l_col * l_row
        w_row = jnp.sum(jnp.where(rid == k, r, 0.0), axis=0, keepdims=True) * inv
        below = jnp.where(rid1 > k, l_col, 0.0)
        r = jnp.where(rid == k, w_row, r - below * w_row)
        return s, r

    for j in range(nblk):
        o = j * NB
        s = work[o:o + NB, o:o + NB]
        _, wjj = lax.fori_loop(0, NB, step, (s, eye), unroll=8)
        w_ref[o:o + NB, o:o + NB] = wjj
        if j < nblk - 1:
            lij = _dot_t(work[o + NB:, o:o + NB], wjj)
            work[o + NB:, o:o + NB] = lij
            work[o + NB:, o + NB:] = work[o + NB:, o + NB:] - _dot_t(lij, lij)
    for i in range(1, nblk):
        o = i * NB
        t = _dot(work[o:o + NB, 0:o], w_ref[0:o, 0:o])
        w_ref[o:o + NB, 0:o] = -_dot(w_ref[o:o + NB, o:o + NB], t)


def inv_chol(a):
    n = a.shape[0]
    return pl.pallas_call(
        _inv_chol_kernel,
        out_shape=jax.ShapeDtypeStruct((n, n), jnp.float32),
        in_specs=[pl.BlockSpec(memory_space=pltpu.VMEM)],
        out_specs=pl.BlockSpec(memory_space=pltpu.VMEM),
        scratch_shapes=[pltpu.VMEM((n, n), jnp.float32)],
    )(a)


B = 1024


def broadcast(array, axis, root):
    mine = lax.axis_index(axis) == root
    return lax.psum(jnp.where(mine, array, jnp.zeros_like(array)), axis)


def per_device(gradients, ridge, panel_index, block_ids):
    local_rows = gradients.shape[0]
    blocks_here = local_rows // B
    ids = jnp.arange(block_ids.shape[0], dtype=jnp.int32)
    position = jnp.sum(jnp.where(block_ids == panel_index[0], ids, 0))
    owner = position // blocks_here
    offset = position % blocks_here * B
    own_tile = lax.dynamic_slice_in_dim(gradients, offset, B, 0)
    pivot = broadcast(own_tile, "rows", owner)
    numbers = (((1,), (1,)), ((), ()))
    share = local_rows // lax.axis_size("dims")

    rows_n = lax.axis_size("rows")
    core = lax.axis_index("rows") % 2
    half = B // 2
    mine = lax.dynamic_slice_in_dim(pivot, core * half, half, 0)
    tile_half = lax.psum(
        lax.dot_general(
            mine, pivot, numbers, precision=lax.Precision.HIGH, preferred_element_type=jnp.float32
        ),
        "dims",
    )
    other_half = lax.ppermute(tile_half, "rows", [(i, i ^ 1) for i in range(rows_n)])
    tile = jnp.where(
        core == 0,
        jnp.concatenate([tile_half, other_half], axis=0),
        jnp.concatenate([other_half, tile_half], axis=0),
    )

    column = lax.psum_scatter(
        lax.dot_general(
            gradients,
            pivot,
            numbers,
            precision=lax.Precision.HIGH,
            preferred_element_type=jnp.float32,
        ),
        "dims",
        scatter_dimension=0,
        tiled=True,
    )
    first = lax.axis_index("rows") * local_rows + lax.axis_index("dims") * share
    row_ids = first + jnp.arange(share, dtype=jnp.int32)[:, None]
    col_ids = position * B + jnp.arange(B, dtype=jnp.int32)[None, :]
    column = column + jnp.where(row_ids == col_ids, ridge, jnp.float32(0.0))
    inverse = inv_chol(tile + ridge * jnp.eye(B, dtype=jnp.float32))
    return _dot_high(column, inverse)


def solution(mesh):
    in_specs = (P("rows", "dims"), P(), P(), P())
    out_specs = P(("rows", "dims"), None)
    return jax.shard_map(
        per_device, mesh=mesh, in_specs=in_specs, out_specs=out_specs, check_vma=False
    )
```

profile of v0, /device:TPU:1, one launch (start us, length us, event | category | flops | bytes accessed | tf_op | source)
XLA Modules:
  0.0 379.3 jit_solution(10874581077007172248)
XLA Ops:
  6.5 0.0 all-reduce.3.cloned.1.call-start
  7.2 1.3 fusion.11
  10.8 5.0 %dynamic-slice_select_fusion = f32[1024,1024]{1,0:T(8,128)} fusion(f32[2048,1024]{1,0:T(8,128)} %param.4, s32[]{:T(128)S(6)} %select_n.47, pred[]{:T(512)S(6)} %eq.33), kind=kLoop, calls=%fused_computation.4 | loop fusion | flops 1048576 | bytes 8388613 | tf_op jit(solution)/shard_map/jit(_where)/select_n | solution.py:82
  15.8 0.0 all-reduce.3.cloned.1.call-update
  15.8 0.0 all-reduce.5.cloned.1.call-start
  15.8 114.7 %all-reduce.3.cloned.1.call-done = f32[1024,1024]{1,0:T(8,128)} async-done(((f32[1024,1024]{1,0:T(8,128)}), f32[1024,1024]{1,0:T(8,128)}) %all-reduce.3.cloned.1.call-update) | async-done | bytes 4194320 | tf_op jit(solution)/shard_map/psum | solution.py:82
  130.5 7.6 %fusion.1 = f32[512,1024]{1,0:T(8,128)} fusion(f32[1024,1024]{1,0:T(8,128)} %all-reduce.3.cloned.1.call-done, s32[]{:T(128)S(6)} %select_n.52), kind=kOutput, calls=%fused_computation.5 | convolution fusion | flops 3221225472 | bytes 8388612 | tf_op jit(solution)/shard_map/dot_general | solution.py:102
  138.2 0.0 all-reduce.5.cloned.1.call-update
  138.2 0.0 reduce-scatter.2.cloned.1.call-start
  138.3 18.1 %convolution_bitcast_fusion = f32[2048,1024]{0,1:T(8,128)} fusion(f32[1024,1024]{1,0:T(8,128)} %all-reduce.3.cloned.1.call-done, f32[2048,1024]{1,0:T(8,128)} %param.4), kind=kOutput, calls=%fused_computation | convolution fusion | flops 12884901888 | bytes 20971520 | tf_op jit(solution)/shard_map/dot_general | solution.py:115
  156.4 0.0 reduce-scatter.2.cloned.1.call-update
  156.4 40.4 %all-reduce.5.cloned.1.call-done = f32[512,1024]{1,0:T(8,128)} async-done(((f32[512,1024]{1,0:T(8,128)}), f32[512,1024]{1,0:T(8,128)}) %all-reduce.5.cloned.1.call-update) | async-done | bytes 2097168 | tf_op jit(solution)/shard_map/psum | solution.py:101
  196.8 1.1 collective-permute-start
  199.1 2.7 collective-permute-done
  201.9 4.2 %fusion.a_ref = f32[1024,1024]{1,0:T(8,128)} fusion(f32[512,1024]{1,0:T(8,128)S(1)} %collective-permute-done, f32[512,1024]{1,0:T(8,128)} %all-reduce.5.cloned.1.call-done, f32[]{:T(128)S(6)} %copy.7, pred[]{:T(512)S(6)} %eq.37), kind=kLoop, calls=%fused_computation.2 | loop fusion | flops 6291456 | bytes 8388613 | tf_op jit(solution)/shard_map/add | solution.py:130
  206.0 155.6 %shard_map.46 = f32[1024,1024]{1,0:T(8,128)} custom-call(f32[1024,1024]{1,0:T(8,128)} %fusion.a_ref), custom_call_target="tpu_custom_call" | custom-call | tf_op jit(solution)/shard_map/pallas_call | solution.py:68
  361.6 0.0 reduce-scatter.2.cloned.1.call-done
  361.6 11.0 %fusion.3 = f32[512,1024]{1,0:T(8,128)} fusion(f32[1024,1024]{1,0:T(8,128)} %shard_map.46, f32[512,1024]{0,1:T(8,128)} %reduce-scatter.2.cloned.1.call-done, f32[]{:T(128)S(6)} %copy.7, s32[512]{0:T(512)S(1)} %iota_add_fusion.1, s32[1024]{0:T(1024)S(1)} %iota_add_fusion), kind=kOutput, calls=%fused_computation.7 | convolution fusion | flops 3222798336 | bytes 8394756 | tf_op jit(solution)/shard_map/dot_general | solution.py:17
  (2 shorter events, 0.0 us)
Async XLA Ops:
  6.5 124.0 %all-reduce.3.cloned.1.call-start = ((), (), s32[]{:S(2)}) async-start(), calls=%async_computation.1 | async-start | bytes 8388608 | tf_op jit(solution)/shard_map/psum | solution.py:82
  15.8 181.0 %all-reduce.5.cloned.1.call-start = ((), (), s32[]{:S(2)}) async-start(), calls=%async_computation.3 | async-start | bytes 4194304 | tf_op jit(solution)/shard_map/psum | solution.py:101
  138.2 223.4 %reduce-scatter.2.cloned.1.call-start = ((), (), s32[]{:S(2)}) async-start(), calls=%async_computation.2 | async-start | bytes 10485760 | tf_op jit(solution)/shard_map/reduce_scatter | solution.py:114
  196.8 5.1 %collective-permute-start = (f32[512,1024]{1,0:T(8,128)}, f32[512,1024]{1,0:T(8,128)S(1)}, u32[]{:S(2)}, u32[]{:S(2)}) collective-permute-start(f32[512,1024]{1,0:T(8,128)} %all-reduce.5.cloned.1.call-done), channel_id=1, source_target_pairs={{0,4},{4,0},{8,12},{12,8},{16,20},{20,16},{24,28},{28,24},{32,36},... | collective-permute-start | bytes 6291464 | tf_op jit(solution)/shard_map/ppermute | solution.py:107
Sparse Core Ops, SparseCore 0:
  15.9 114.5 all-reduce.2
  138.3 58.4 all-reduce.4
  199.3 80.5 reduce-scatter.1
where the time goes:
time: 386 us; the launch traced here: 379 us
  waiting for transfers between devices  158 us (41%)
  Pallas kernels  156 us (40%)
  matrix products  36.8 us (10%)
  between operations  17.5 us (5%)
  other arithmetic  10.4 us (3%)
    pallas_call x1, Pallas kernels, inv_chol(): pl.pallas_call(_inv_chol_kernel, out_shape=jax.ShapeDtypeStruct((n, n), j...  156 us
    psum x1, waiting for transfers between devices, broadcast(): return lax.psum(jnp.where(mine, array, jnp.zeros_like(array)), axis)  115 us
    psum x1, waiting for transfers between devices, per_device(): lax.psum(lax.dot_general(mine, pivot, numbers, precision=lax.Precision.HI...  40.4 us
    dot_general x1, matrix products, per_device(): lax.dot_general(gradients, pivot, numbers, precision=lax.Precision.HIGH,...  18.1 us
    dot_general x1, matrix products, _dot_high(): lax.dot_general(a, b, (((1,), (1,)), ((), ())), precision=lax.Precision.H...  11 us
  transfers between devices with their start and end apart: 4, of which 3 were waited for; matrix products, arithmetic and copies ran while one was open for 6% of the time, Pallas kernels for 41%

commit v1 on v0

--- a/solution.py
+++ b/solution.py
@@ -97,18 +97,34 @@
     rows_n = lax.axis_size("rows")
     core = lax.axis_index("rows") % 2
     half = B // 2
-    mine = lax.dynamic_slice_in_dim(pivot, core * half, half, 0)
-    tile_half = lax.psum(
-        lax.dot_general(
-            mine, pivot, numbers, precision=lax.Precision.HIGH, preferred_element_type=jnp.float32
-        ),
-        "dims",
-    )
-    other_half = lax.ppermute(tile_half, "rows", [(i, i ^ 1) for i in range(rows_n)])
-    tile = jnp.where(
-        core == 0,
-        jnp.concatenate([tile_half, other_half], axis=0),
-        jnp.concatenate([other_half, tile_half], axis=0),
+    r_ids = lax.broadcasted_iota(jnp.int32, (half, half), 0)
+    c_ids = lax.broadcasted_iota(jnp.int32, (half, half), 1)
+    top, bottom = pivot[:half], pivot[half:]
+
+    def lower_left():
+        x = _dot_high(bottom, top)
+        return jnp.concatenate([x, jnp.zeros((8, half), jnp.float32)], axis=0)
+
+    def diagonal_pair():
+        t00 = _dot_high(top, top)
+        t11 = _dot_high(bottom, bottom)
+        m = jnp.where(r_ids >= c_ids, t00, t11)
+        d11 = jnp.sum(jnp.where(r_ids == c_ids, t11, 0.0), axis=0, keepdims=True)
+        return jnp.concatenate([m, jnp.broadcast_to(d11, (8, half))], axis=0)
+
+    reduced = lax.psum(lax.cond(core == 0, lower_left, diagonal_pair), "dims")
+    swapped = lax.ppermute(reduced, "rows", [(i, i ^ 1) for i in range(rows_n)])
+    quarter_x = jnp.where(core == 0, reduced, swapped)[:half]
+    packed = jnp.where(core == 0, swapped, reduced)
+    m, d11 = packed[:half], packed[half:half + 1]
+    t00 = jnp.where(r_ids >= c_ids, m, m.T)
+    t11 = jnp.where(r_ids < c_ids, m, jnp.where(r_ids > c_ids, m.T, d11))
+    tile = jnp.concatenate(
+        [
+            jnp.concatenate([t00, jnp.zeros((half, half), jnp.float32)], axis=1),
+            jnp.concatenate([quarter_x, t11], axis=1),
+        ],
+        axis=0,
     )
 
     column = lax.psum_scatter(

time: 386 us -> 375 us (0.972)
  waiting for transfers between devices: 158 us -> 142 us
  local copies, waits for them, and re-layouts: 0 us -> 7.27 us
  matrix products: 36.8 us -> 32.9 us
    psum x1, waiting for transfers between devices: 40.4 us -> 26.4 us  [per_device(): reduced = lax.psum(lax.cond(core == 0, lower_left, diagonal_pair), 'dims')]
    dot_general x1 -> x0, matrix products: 7.64 us -> none  [per_device(): lax.dot_general(mine, pivot, numbers, precision=lax.Precision.HIGH, prefe...]
    slice x0 -> x4, local copies, waits for them, and re-layouts: none -> 6.11 us  [the longest x3 3.58 us: per_device(): m, d11 = (packed[:half], packed[half:half + 1])]
    dot_general x1 -> x3, matrix products: 11 us -> 14.8 us  [_dot_high(): lax.dot_general(a, b, (((1,), (1,)), ((), ())), precision=lax.Precision.H...]
  transfers between devices with their start and end apart: 4 -> 4, of which waited for: 3 -> 3; matrix products, arithmetic and copies ran while one was open for 6% -> 7% of each run, Pallas kernels for 41% -> 42%
where the time goes in v1:
time: 375 us; the launch traced here: 372 us
  Pallas kernels  157 us (42%)
  waiting for transfers between devices  142 us (38%)
  matrix products  32.9 us (9%)
  between operations  17.5 us (5%)
  other arithmetic  11.8 us (3%)
  local copies, waits for them, and re-layouts  7.27 us (2%)
    pallas_call x1, Pallas kernels, inv_chol(): pl.pallas_call(_inv_chol_kernel, out_shape=jax.ShapeDtypeStruct((n, n), j...  157 us
    psum x1, waiting for transfers between devices, broadcast(): return lax.psum(jnp.where(mine, array, jnp.zeros_like(array)), axis)  115 us
    psum x1, waiting for transfers between devices, per_device(): reduced = lax.psum(lax.cond(core == 0, lower_left, diagonal_pair), 'dims')  26.4 us
    dot_general x1, matrix products, per_device(): lax.dot_general(gradients, pivot, numbers, precision=lax.Precision.HIGH,...  18.2 us
    dot_general x3, matrix products, _dot_high(): lax.dot_general(a, b, (((1,), (1,)), ((), ())), precision=lax.Precision.H...  14.8 us
  transfers between devices with their start and end apart: 4, of which 3 were waited for; matrix products, arithmetic and copies ran while one was open for 7% of the time, Pallas kernels for 42%

profile of v1, /device:TPU:1, one launch (start us, length us, event | category | flops | bytes accessed | tf_op | source)
XLA Modules:
  0.0 371.6 jit_solution(13898053280364817574)
XLA Ops:
  6.5 0.0 all-reduce.5.cloned.1.call-start
  7.2 1.3 fusion.10
  10.7 5.0 %dynamic-slice_select_fusion = f32[1024,1024]{1,0:T(8,128)} fusion(f32[2048,1024]{1,0:T(8,128)} %param.6, s32[]{:T(128)S(6)} %select_n.68, pred[]{:T(512)S(6)} %eq.38), kind=kLoop, calls=%fused_computation.8 | loop fusion | flops 1048576 | bytes 8388613 | tf_op jit(solution)/shard_map/jit(_where)/select_n | solution.py:82
  15.6 0.0 all-reduce.5.cloned.1.call-update
  15.6 0.0 all-reduce.7.cloned.1.call-start
  15.7 114.7 %all-reduce.5.cloned.1.call-done = f32[1024,1024]{1,0:T(8,128)} async-done(((f32[1024,1024]{1,0:T(8,128)}), f32[1024,1024]{1,0:T(8,128)}) %all-reduce.5.cloned.1.call-update) | async-done | bytes 4194320 | tf_op jit(solution)/shard_map/psum | solution.py:82
  130.4 2.5 fusion.12
  132.9 0.1 iota.54
  133.0 0.1 iota.55
  133.1 3.9 %conditional.1 = (f32[520,512]{1,0:T(8,128)S(1)}) conditional(s32[]{:T(128)} %convert_element_type.4, (s32[512,512]{1,0:T(8,128)S(1)}, s32[512,512]{1,0:T(8,128)S(1)}, f32[512,1024]{1,0:T(8,128)S(1)}, f32[512,1024]{1,0:T(8,128)S(1)}, s32[512,512]{1,0:T(8,128)S(1)}, /*index=5*/s32[512,512]{1,0:T(8,128)S(1)}) %tuple.11, (f32[512,1024]{1,0:T(8,128)S(1)}, ...), branch_computations={%region_3.5_spmd, %region_5.6_spmd} | conditional | flops 3222801920 | bytes 13684744 | solution.py:115
  133.2 1.9 select_reduce_fusion
  135.0 1.9 convolution_select_fusion
  136.9 0.1 pad_maximum_fusion
  137.0 0.0 copy-start
  137.0 1.0 copy-done
  138.0 0.0 all-reduce.7.cloned.1.call-update
  138.0 0.0 reduce-scatter.2.cloned.1.call-start
  138.1 18.2 %convolution_bitcast_fusion = f32[2048,1024]{0,1:T(8,128)} fusion(f32[1024,1024]{1,0:T(8,128)} %all-reduce.5.cloned.1.call-done, f32[2048,1024]{1,0:T(8,128)} %param.6), kind=kOutput, calls=%fused_computation.3 | convolution fusion | flops 12884901888 | bytes 20971520 | tf_op jit(solution)/shard_map/dot_general | solution.py:131
  156.2 0.0 reduce-scatter.2.cloned.1.call-update
  156.2 26.4 %all-reduce.7.cloned.1.call-done = f32[520,512]{1,0:T(8,128)} async-done(((f32[520,512]{1,0:T(8,128)}), f32[520,512]{1,0:T(8,128)}) %all-reduce.7.cloned.1.call-update) | async-done | bytes 1064976 | tf_op jit(solution)/shard_map/psum | solution.py:115
  182.6 2.3 collective-permute-start
  186.1 1.3 collective-permute-done
  187.4 1.4 broadcast_select_fusion
  188.8 0.0 copy-start.1
  188.9 1.0 slice.22
  189.9 2.5 copy.5
  192.4 0.0 copy-done.1
  192.4 1.7 fusion.5
  194.1 2.4 fusion.a_ref
  196.5 157.4 %shard_map.46 = f32[1024,1024]{1,0:T(8,128)} custom-call(f32[1024,1024]{1,0:T(8,128)} %fusion.a_ref), custom_call_target="tpu_custom_call" | custom-call | tf_op jit(solution)/shard_map/pallas_call | solution.py:68
  353.9 0.0 reduce-scatter.2.cloned.1.call-done
  353.9 11.0 %fusion.1 = f32[512,1024]{1,0:T(8,128)} fusion(f32[1024,1024]{1,0:T(8,128)} %shard_map.46, f32[512,1024]{0,1:T(8,128)} %reduce-scatter.2.cloned.1.call-done, f32[]{:T(128)S(6)} %copy.10, s32[512]{0:T(512)S(1)} %iota_add_fusion.1, s32[1024]{0:T(1024)S(1)} %iota_add_fusion), kind=kOutput, calls=%fused_computation.9 | convolution fusion | flops 3222798336 | bytes 8394756 | tf_op jit(solution)/shard_map/dot_general | solution.py:17
  (4 shorter events, 0.0 us)
Async XLA Ops:
  6.5 123.9 %all-reduce.5.cloned.1.call-start = ((), (), s32[]{:S(2)}) async-start(), calls=%async_computation.1 | async-start | bytes 8388608 | tf_op jit(solution)/shard_map/psum | solution.py:82
  15.6 167.0 %all-reduce.7.cloned.1.call-start = ((), (), s32[]{:S(2)}) async-start(), calls=%async_computation.3 | async-start | bytes 2129920 | tf_op jit(solution)/shard_map/psum | solution.py:115
  137.0 1.0 copy-start
  138.0 215.9 %reduce-scatter.2.cloned.1.call-start = ((), (), s32[]{:S(2)}) async-start(), calls=%async_computation.2 | async-start | bytes 10485760 | tf_op jit(solution)/shard_map/reduce_scatter | solution.py:130
  182.6 4.8 %collective-permute-start = (f32[520,512]{1,0:T(8,128)}, f32[520,512]{1,0:T(8,128)S(1)}, u32[]{:S(2)}, u32[]{:S(2)}) collective-permute-start(f32[520,512]{1,0:T(8,128)} %all-reduce.7.cloned.1.call-done), channel_id=1, source_target_pairs={{0,4},{4,0},{8,12},{12,8},{16,20},{20,16},{24,28},{28,24},{32,36},... | collective-permute-start | bytes 3194888 | tf_op jit(solution)/shard_map/ppermute | solution.py:116
  188.8 3.6 copy-start.1
Sparse Core Ops, SparseCore 0:
  15.8 114.5 all-reduce.4
  138.1 44.4 all-reduce.6
  185.1 83.0 reduce-scatter.1
